TPU v7x, 32 devices: a whole 2x2x4 slice. The times are simulated.
32 devices in a mesh: groups: 1, blk: 8 (over z, y), seg: 2 (over x), freq: 2 (over core).
Axes of the slice: x: 2, y: 2, z: 4, core: 2. Of those that a mesh axis runs over, the one named last changes fastest.
Arguments:
- raw: bfloat16 [64, 64, 16384], P(('groups', 'blk'), 'seg', 'freq'), may hold values from -6 to 6
- taps: float32 [128], replicated, may hold values from -0.5 to 0.5
- send_list: int32 [8, 8, 2], P(('groups', 'blk')), may hold values from 0 to 8, as said below
- recv_row: int32 [8, 8, 2], P(('groups', 'blk')), may hold values from 0 to 16, as said below
Outputs:
- cross_spectra: float32 [2, 256, 128, 128], P(None, ('seg', 'freq'), ('groups', 'blk'))
Inputs may be any that keep to these rules, and one draw needn't show every extreme that they name: send_list[s, o, k] is the local sensing point of source s that goes to owner o in slot k, or 8 for an empty slot; a source names each of its points at most once; the filled slots of a pair come first; some source fills all 2 slots to one owner. recv_row[o, s, k] is the row of owner o that receives slot k of source s, and it is 16 exactly where send_list[s, o, k] is 8; an owner's filled rows are 0 to its count - 1, each once, rising with source and then slot; some owner holds exactly 16 rows.
All inputs are finite; a program needn't handle non-finite values.
Results may differ from a plain program's by a relative error of at most 0.0029.
Values may be sent and summed in bfloat16 or wider, within the bound.
No kernel may reach another device: no remote copies, remote signals or barrier semaphores. Data moves between devices by JAX's collectives and lax.ppermute only.
A program may use at most 128 MiB of HBM per device.

v0:
```python
import math
import jax
import jax.numpy as jnp
from jax import lax
from jax.sharding import PartitionSpec as P

SEG_LEN = 16384
BINS = 256
BAND_LO = 128
HW = 4
OWN = 16
WHITEN_FLOOR = 0.25
TWO_PI = 2.0 * math.pi


def swapped(value, axis, distance):
    mask = 2**distance
    pairs = [(source, source ^ mask) for source in range(lax.axis_size(axis))]
    return lax.ppermute(value, axis, pairs)


def dft_tables(band_index, sample_index):
    wavenumber = BAND_LO + band_index
    phase_int = wavenumber[:, None] * sample_index[None, :] % SEG_LEN
    angles = phase_int.astype(jnp.float32) * (TWO_PI / SEG_LEN)
    norm_scale = 1.0 / math.sqrt(SEG_LEN)
    cos_part = (jnp.cos(angles) * norm_scale).astype(jnp.bfloat16)
    sin_part = (-jnp.sin(angles) * norm_scale).astype(jnp.bfloat16)
    return (cos_part, sin_part)


def dft_tables_fast(band_index, first_sample, count):
    lanes = 128
    wavenumber = BAND_LO + band_index
    coarse = first_sample + lanes * jnp.arange(count // lanes, dtype=jnp.int32)
    fine = jnp.arange(lanes, dtype=jnp.int32)
    coarse_angle = (wavenumber[:, None] * coarse[None, :] % SEG_LEN).astype(jnp.float32) * (
        TWO_PI / SEG_LEN
    )
    fine_angle = (wavenumber[:, None] * fine[None, :] % SEG_LEN).astype(jnp.float32) * (
        TWO_PI / SEG_LEN
    )
    cos_a = jnp.cos(coarse_angle)[:, :, None]
    sin_a = jnp.sin(coarse_angle)[:, :, None]
    cos_b = jnp.cos(fine_angle)[:, None, :]
    sin_b = jnp.sin(fine_angle)[:, None, :]
    norm_scale = 1.0 / math.sqrt(SEG_LEN)
    cos_sum = cos_a * cos_b - sin_a * sin_b
    sin_sum = sin_a * cos_b + cos_a * sin_b
    rows = band_index.shape[0]
    cos_part = (cos_sum * norm_scale).astype(jnp.bfloat16).reshape(rows, count)
    sin_part = (-sin_sum * norm_scale).astype(jnp.bfloat16).reshape(rows, count)
    return (cos_part, sin_part)


def response(band_index, taps):
    wavenumber = BAND_LO + band_index
    lag_index = jnp.arange(taps.shape[0], dtype=jnp.int32)
    phase_int = wavenumber[:, None] * lag_index[None, :] % SEG_LEN
    angles = phase_int.astype(jnp.float32) * (TWO_PI / SEG_LEN)
    real_part = jnp.dot(jnp.cos(angles), taps, precision=lax.Precision.HIGHEST)
    imag_part = jnp.dot(-jnp.sin(angles), taps, precision=lax.Precision.HIGHEST)
    return (real_part, imag_part)


def per_device(raw, taps, send_list, recv_row):
    owners_count = lax.axis_size("blk")
    seg_count = lax.axis_size("seg")
    freq_count = lax.axis_size("freq")
    freq_rank = lax.axis_index("freq")
    sections, seg_dev, half_len = raw.shape
    records = raw.reshape(sections * seg_dev, half_len)
    device_bins = BINS // freq_count
    block_bins = device_bins // seg_count
    capacity = send_list.shape[2]

    def band_of(row_ids):
        owner_core = row_ids // device_bins
        local_row = row_ids % device_bins
        return (
            local_row // block_bins * freq_count + owner_core
        ) * block_bins + local_row % block_bins

    band_rows = band_of(jnp.arange(device_bins * freq_count, dtype=jnp.int32))
    cos_part, sin_part = dft_tables_fast(band_rows, freq_rank * half_len, half_len)
    contract = (((1,), (1,)), ((), ()))
    real_all = lax.dot_general(cos_part, records, contract, preferred_element_type=jnp.float32)
    imag_all = lax.dot_general(sin_part, records, contract, preferred_element_type=jnp.float32)
    blocks = jnp.stack([real_all, imag_all], axis=1)
    blocks = blocks.reshape(freq_count, device_bins, 2, records.shape[0])
    if freq_count == 2:
        kept = jnp.where(freq_rank == 0, blocks[0], blocks[1])
        sent = jnp.where(freq_rank == 0, blocks[1], blocks[0])
        spectra = kept + swapped(sent, "freq", 0)
    else:
        spectra = lax.psum_scatter(
            blocks.reshape(device_bins * freq_count, 2, records.shape[0]),
            "freq",
            scatter_dimension=0,
            tiled=True,
        )
    real_part = spectra[:, 0]
    imag_part = spectra[:, 1]
    amplitude = jnp.sqrt(real_part * real_part + imag_part * imag_part + 1e-06)
    amp_blocks = amplitude.reshape(seg_count, block_bins, -1)
    band_rims = jnp.stack([amp_blocks[:, :HW], amp_blocks[:, block_bins - HW :]])
    partner = swapped(band_rims, "freq", 0)
    zero_rim = jnp.zeros_like(partner[1][:1])
    right_prev = jnp.concatenate([zero_rim, partner[1][:-1]], axis=0)
    left_next = jnp.concatenate([partner[0][1:], zero_rim], axis=0)
    first_core = freq_rank == 0
    lower_rim = jnp.where(first_core, right_prev, partner[1])
    upper_rim = jnp.where(first_core, partner[0], left_next)
    padded = jnp.concatenate([lower_rim, amp_blocks, upper_rim], axis=1)
    window_sum = padded[:, 0:block_bins]
    for offset_step in range(1, 2 * HW + 1):
        window_sum = window_sum + padded[:, offset_step : offset_step + block_bins]
    span_ids = jnp.arange(seg_count, dtype=jnp.int32)[:, None]
    offsets = jnp.arange(block_bins, dtype=jnp.int32)[None, :]
    position = (span_ids * freq_count + freq_rank) * block_bins + offsets
    counted = jnp.minimum(position + HW, BINS - 1) - jnp.maximum(position - HW, 0) + 1
    smooth = window_sum / counted.astype(jnp.float32)[:, :, None]
    divisor = jnp.maximum(smooth, WHITEN_FLOOR).reshape(device_bins, -1)
    local_bins = freq_rank * device_bins + jnp.arange(device_bins, dtype=jnp.int32)
    response_re, response_im = response(band_of(local_bins), taps)
    scaled_re = real_part / divisor
    scaled_im = imag_part / divisor
    white_re = scaled_re * response_re[:, None] - scaled_im * response_im[:, None]
    white_im = scaled_re * response_im[:, None] + scaled_im * response_re[:, None]
    whitened = jnp.stack([white_re, white_im], axis=1).astype(jnp.bfloat16)
    whitened = whitened.reshape(device_bins, 2, sections, seg_dev)
    slot_ids = send_list.reshape(-1)
    picker = (slot_ids[:, None] == jnp.arange(sections, dtype=jnp.int32)[None, :]).astype(
        jnp.bfloat16
    )
    packed = jnp.einsum(
        "pc,fxcn->pxnf", picker, whitened, preferred_element_type=jnp.float32
    ).astype(jnp.bfloat16)
    packed = packed.reshape(owners_count, capacity, 2, seg_dev, device_bins)
    arrived = lax.all_to_all(packed, "blk", split_axis=0, concat_axis=0, tiled=True)
    arrived = arrived.reshape(owners_count * capacity, 2, seg_dev, device_bins)
    row_targets = recv_row.reshape(-1)
    placer = (jnp.arange(OWN, dtype=jnp.int32)[:, None] == row_targets[None, :]).astype(
        jnp.bfloat16
    )
    own_block = jnp.einsum(
        "rp,pxnf->xnrf", placer, arrived, preferred_element_type=jnp.float32
    ).astype(jnp.bfloat16)
    incoming = lax.all_gather(own_block, "blk", axis=2, tiled=True)
    cross_re = jnp.einsum("xnif,xnjf->fij", own_block, incoming, preferred_element_type=jnp.float32)
    cross_im = jnp.einsum(
        "nif,njf->fij", own_block[1], incoming[0], preferred_element_type=jnp.float32
    )
    cross_im = cross_im - jnp.einsum(
        "nif,njf->fij", own_block[0], incoming[1], preferred_element_type=jnp.float32
    )
    pair_block = jnp.stack([cross_re, cross_im])
    stacked = lax.psum_scatter(pair_block, "seg", scatter_dimension=1, tiled=True)
    return stacked / jnp.float32(seg_dev * seg_count)


def solution(mesh):
    placed = (
        P(("groups", "blk"), "seg", "freq"),
        P(),
        P(("groups", "blk"), None, None),
        P(("groups", "blk"), None, None),
    )
    return jax.shard_map(
        per_device,
        mesh=mesh,
        in_specs=placed,
        out_specs=P(None, ("seg", "freq"), ("groups", "blk"), None),
        check_vma=False,
    )
```

profile of v0, /device:TPU:0, one launch (start us, length us, event | category | flops | bytes accessed | tf_op | source)
XLA Modules:
  0.0 164.3 jit_solution(13299411521968200792)
XLA Ops:
  6.6 0.6 fusion.52
  7.2 0.6 fusion.54
  7.8 5.0 %multiply_convert_fusion.1 = (bf16[256,64,128]{2,1,0:T(8,128)(2,1)S(1)}, bf16[256,64,128]{2,1,0:T(8,128)(2,1)S(1)}) fusion(f32[256,128]{1,0:T(8,128)S(1)} %get-tuple-element.22, f32[256,64]{1,0:T(8,128)S(1)} %get-tuple-element.20, f32[256,128]{1,0:T(8,128)S(1)} %get-tuple-element.21, f32[256,64]{1,0:T(8,128)S(1)} %get-tuple-element.19), kind=kLoop, calls=%fused_computation.1 | loop fusion | flops 23068672 | bytes 8781824 | tf_op jit(solution)/shard_map/convert_element_type | solution.py:51
  12.7 2.9 %fusion.8 = f32[256,1,256]{0,2,1:T(8,128)S(1)} fusion(bf16[256,8192]{1,0:T(8,128)(2,1)S(1)} %bitcast.112, bf16[32,8,64,128]{3,2,1,0:T(8,128)(2,1)S(1)} %bitcast.102), kind=kOutput, calls=%fused_computation.16 | convolution fusion | flops 1073741824 | bytes 8650752 | tf_op jit(solution)/shard_map/dot_general | solution.py:87
  15.6 2.9 %fusion.11 = f32[256,1,256]{0,2,1:T(8,128)S(1)} fusion(bf16[256,8192]{1,0:T(8,128)(2,1)S(1)} %bitcast.113, bf16[32,8,64,128]{3,2,1,0:T(8,128)(2,1)S(1)} %bitcast.101), kind=kOutput, calls=%fused_computation.17 | convolution fusion | flops 1073741824 | bytes 8650752 | tf_op jit(solution)/shard_map/dot_general | solution.py:88
  22.4 1.0 copy.38
  23.4 7.2 %all-to-all-start = ((bf16[8,2,2,32,128]{4,1,3,2,0:T(2,128)(2,1)}), bf16[8,2,2,32,128]{4,1,3,2,0:T(2,128)(2,1)S(1)}, u32[]{:S(2)}, u32[]{:S(2)}) async-start(bf16[8,2,2,32,128]{4,1,3,2,0:T(2,128)(2,1)} %copy.38), calls=%async_computation | async-start | bytes 524288 | tf_op jit(solution)/shard_map/all_to_all | solution.py:140
  30.8 9.0 %all-to-all-done = bf16[8,2,2,32,128]{4,1,3,2,0:T(2,128)(2,1)S(1)} async-done(((bf16[8,2,2,32,128]{4,1,3,2,0:T(2,128)(2,1)}), bf16[8,2,2,32,128]{4,1,3,2,0:T(2,128)(2,1)S(1)}, u32[]{:S(2)}, u32[]{:S(2)}) %all-to-all-start) | async-done | bytes 262176 | tf_op jit(solution)/shard_map/all_to_all | solution.py:140
  40.0 0.9 fusion.7
  41.2 2.7 %copy.41 = bf16[2,32,16,128]{1,2,0,3:T(8,128)(2,1)S(1)} copy(bf16[2,32,16,128]{3,2,1,0:T(8,128)(2,1)} %fusion.7) | data formatting | bytes 524288 | tf_op jit(solution)/shard_map/convert_element_type | solution.py:148
  43.8 1.0 slice_bitcast_fusion.2
  44.8 1.2 copy.45
  46.1 1.2 copy.43
  47.3 43.8 %all-gather.2.cloned.1.call-done = bf16[2,32,128,128]{3,2,1,0:T(8,128)(2,1)} async-done(((bf16[2,32,16,128]{3,2,1,0:T(8,128)(2,1)}), bf16[2,32,128,128]{3,2,1,0:T(8,128)(2,1)}) %all-gather.2.cloned.1.call-update) | async-done | bytes 2097168 | tf_op jit(solution)/shard_map/all_gather | solution.py:149
  91.2 3.1 %slice_bitcast_fusion = (bf16[32,128,128]{2,1,0:T(8,128)(2,1)}, bf16[32,128,128]{2,1,0:T(8,128)(2,1)}) fusion(bf16[2,32,128,128]{3,2,1,0:T(8,128)(2,1)} %all-gather.2.cloned.1.call-done), kind=kLoop, calls=%fused_computation.20 | loop fusion | bytes 4194304 | tf_op jit(solution)/shard_map/squeeze | solution.py:155
  94.3 2.8 %copy.46 = bf16[32,128,128]{1,0,2:T(8,128)(2,1)} copy(bf16[32,128,128]{2,1,0:T(8,128)(2,1)} %get-tuple-element.5) | data formatting | bytes 2097152 | tf_op jit(solution)/shard_map/squeeze | solution.py:155
  97.1 2.6 %copy.44 = bf16[32,128,128]{1,0,2:T(8,128)(2,1)} copy(bf16[32,128,128]{2,1,0:T(8,128)(2,1)} %get-tuple-element.6) | data formatting | bytes 2097152 | tf_op jit(solution)/shard_map/squeeze | solution.py:152
  99.7 2.8 %fusion.85 = f32[128,16,128]{2,1,0:T(8,128)} fusion(bf16[32,16,128]{0,1,2:T(8,128)(2,1)} %copy.43, bf16[32,128,128]{1,0,2:T(8,128)(2,1)} %copy.44), kind=kOutput, calls=%fused_computation.159 | convolution fusion | flops 16777216 | bytes 2228224 | tf_op jit(solution)/shard_map/nif,njf->fij/dot_general | solution.py:151
  102.5 12.6 %copy.42 = bf16[2,32,128,128]{1,2,0,3:T(8,128)(2,1)} copy(bf16[2,32,128,128]{3,2,1,0:T(8,128)(2,1)S(1)} %copy-done.1) | data formatting | bytes 4194304 | tf_op jit(solution)/shard_map/all_gather | solution.py:149
  115.1 5.8 %convolution_bitcast_fusion = f32[1,128,16,128]{3,2,1,0:T(8,128)S(1)} fusion(bf16[2,32,16,128]{1,2,0,3:T(8,128)(2,1)S(1)} %copy.41, bf16[2,32,128,128]{1,2,0,3:T(8,128)(2,1)} %copy.42), kind=kOutput, calls=%fused_computation.12 | convolution fusion | flops 33554432 | bytes 3407872 | tf_op jit(solution)/shard_map/xnif,xnjf->fij/dot_general | solution.py:150
  121.8 3.0 %copy.70 = f32[16,8,32,128]{3,1,2,0:T(8,128)} copy(f32[16,8,32,128]{3,2,1,0:T(8,128)S(1)} %bitcast.100) | data formatting | bytes 4194304
  124.8 30.2 %reduce-scatter.5.cloned.1.call-done = f32[64,4096]{1,0:T(8,128)} async-done(((f32[128,4096]{1,0:T(8,128)}), f32[64,4096]{1,0:T(8,128)}) %reduce-scatter.5.cloned.1.call-update) | async-done | bytes 1048592
  155.0 1.4 copy.55
  156.4 1.1 copy_multiply_fusion
  (53 shorter events, 5.4 us)
Async XLA Ops:
  6.5 12.6 %copy-start = (f32[128]{0:T(128)S(1)}, f32[128]{0:T(128)}, u32[]{:S(2)}) copy-start(f32[128]{0:T(128)} %param.5) | copy-start | bytes 1540
  7.8 5.0 %copy-start.7 = (bf16[8,32,8192]{2,1,0:T(8,128)(2,1)S(1)}, bf16[8,32,8192]{2,1,0:T(8,128)(2,1)}, u32[]{:S(2)}) copy-start(bf16[8,32,8192]{2,1,0:T(8,128)(2,1)} %param.4) | copy-start | bytes 12582916
  15.6 5.8 %copy-start.5 = (s32[1,8,2]{1,2,0:T(2,128)S(1)}, s32[1,8,2]{1,2,0:T(2,128)}, u32[]{:S(2)}) copy-start(s32[1,8,2]{1,2,0:T(2,128)} %param.6) | copy-start | bytes 196
  18.5 12.1 %copy-start.6 = (s32[1,8,2]{1,2,0:T(2,128)S(1)}, s32[1,8,2]{1,2,0:T(2,128)}, u32[]{:S(2)}) copy-start(s32[1,8,2]{1,2,0:T(2,128)} %param.7) | copy-start | bytes 196
  18.6 1.7 %collective-permute-start = (f32[128,2,256]{0,2,1:T(8,128)S(1)}, f32[128,2,256]{0,2,1:T(8,128)S(1)}, u32[]{:S(2)}, u32[]{:S(2)}) collective-permute-start(f32[128,2,256]{0,2,1:T(8,128)S(1)} %broadcast_select_fusion), channel_id=1, source_target_pairs={{0,1},{1,0},{2,3},{3,2},{4,5},{5,4},{6,7},{7,6},{8,9},{9,8},{10,11... | collective-permute-start | bytes 786440 | tf_op jit(solution)/shard_map/ppermute | solution.py:19
  20.5 1.3 collective-permute-start.1
  23.4 16.4 %all-to-all-start = ((bf16[8,2,2,32,128]{4,1,3,2,0:T(2,128)(2,1)}), bf16[8,2,2,32,128]{4,1,3,2,0:T(2,128)(2,1)S(1)}, u32[]{:S(2)}, u32[]{:S(2)}) async-start(bf16[8,2,2,32,128]{4,1,3,2,0:T(2,128)(2,1)} %copy.38), calls=%async_computation | async-start | bytes 524288 | tf_op jit(solution)/shard_map/all_to_all | solution.py:140
  30.6 60.6 %all-gather.2.cloned.1.call-start = ((), (), s32[]{:S(2)}) async-start(), calls=%async_computation.2 | async-start | bytes 2359296 | tf_op jit(solution)/shard_map/all_gather | solution.py:149
  40.9 114.1 %reduce-scatter.5.cloned.1.call-start = ((), (), s32[]{:S(2)}) async-start(), calls=%async_computation.3 | async-start | bytes 3145728
  94.3 8.3 %copy-start.1 = (bf16[2,32,128,128]{3,2,1,0:T(8,128)(2,1)S(1)}, bf16[2,32,128,128]{3,2,1,0:T(8,128)(2,1)}, u32[]{:S(2)}) copy-start(bf16[2,32,128,128]{3,2,1,0:T(8,128)(2,1)} %all-gather.2.cloned.1.call-done) | copy-start | bytes 6291460
  115.1 5.8 %copy-start.2 = (bf16[32,128,128]{1,0,2:T(8,128)(2,1)S(1)}, bf16[32,128,128]{1,0,2:T(8,128)(2,1)}, u32[]{:S(2)}) copy-start(bf16[32,128,128]{1,0,2:T(8,128)(2,1)} %copy.46) | copy-start | bytes 3145732
  115.1 5.8 %copy-start.3 = (f32[128,16,128]{2,1,0:T(8,128)S(1)}, f32[128,16,128]{2,1,0:T(8,128)}, u32[]{:S(2)}) copy-start(f32[128,16,128]{2,1,0:T(8,128)} %fusion.85) | copy-start | bytes 3145732
  115.1 5.8 %copy-start.4 = (bf16[32,16,128]{0,1,2:T(8,128)(2,1)S(1)}, bf16[32,16,128]{0,1,2:T(8,128)(2,1)}, u32[]{:S(2)}) copy-start(bf16[32,16,128]{0,1,2:T(8,128)(2,1)} %copy.45) | copy-start | bytes 393220
Sparse Core Ops, SparseCore 0:
  41.0 50.0 all-gather.1
  125.0 29.9 reduce-scatter.4
where the time goes:
time: 165 us; the launch traced here: 164 us
  waiting for transfers between devices  83.7 us (51%)
  local copies, waits for them, and re-layouts  33.8 us (20%)
  matrix products  16.9 us (10%)
  between operations  13.6 us (8%)
  starting transfers between devices  8.39 us (5%)
  other arithmetic  7.81 us (5%)
    all_gather x1, waiting for transfers between devices, per_device(): incoming = lax.all_gather(own_block, 'blk', axis=2, tiled=True)  43.8 us
    unnamed x3, waiting for transfers between devices  30.2 us
    all_gather x1, local copies, waits for them, and re-layouts, per_device(): incoming = lax.all_gather(own_block, 'blk', axis=2, tiled=True)  12.6 us
    all_to_all x1, waiting for transfers between devices, per_device(): lax.all_to_all(packed, 'blk', split_axis=0, concat_axis=0, tiled=True)  9.02 us
    all_to_all x1, starting transfers between devices, per_device(): lax.all_to_all(packed, 'blk', split_axis=0, concat_axis=0, tiled=True)  7.18 us
    squeeze x2, local copies, waits for them, and re-layouts, per_device(): incoming[1]  5.95 us
    dot_general x1, matrix products, per_device(): jnp.einsum('xnif,xnjf->fij', own_block, incoming, preferred_element_type=...  5.79 us
    unnamed x21, local copies, waits for them, and re-layouts  4.96 us
  transfers between devices with their start and end apart: 5, of which 5 were waited for; matrix products, arithmetic and copies ran while one was open for 5% of the time, Pallas kernels for 0%

commit v1 on v0

--- a/solution.py
+++ b/solution.py
@@ -11,6 +11,27 @@
 OWN = 16
 WHITEN_FLOOR = 0.25
 TWO_PI = 2.0 * math.pi
+
+
+def collect(shard, axis, dim):
+    size, here, rows = (lax.axis_size(axis), lax.axis_index(axis), shard.shape[dim])
+    forward = [(i, (i + 1) % size) for i in range(size)]
+    left = [(i, (i - 1) % size) for i in range(size)]
+    result = jnp.zeros((*shard.shape[:dim], size * rows, *shard.shape[dim + 1 :]), shard.dtype)
+    result = lax.dynamic_update_slice_in_dim(result, shard, here * rows, axis=dim)
+    from_left = from_right = shard
+    half = size // 2
+    for step in range(1, half + 1):
+        from_left = lax.ppermute(from_left, axis, forward)
+        result = lax.dynamic_update_slice_in_dim(
+            result, from_left, (here - step) % size * rows, axis=dim
+        )
+        if step < size - half:
+            from_right = lax.ppermute(from_right, axis, left)
+            result = lax.dynamic_update_slice_in_dim(
+                result, from_right, (here + step) % size * rows, axis=dim
+            )
+    return result
 
 
 def swapped(value, axis, distance):
@@ -146,7 +167,7 @@
     own_block = jnp.einsum(
         "rp,pxnf->xnrf", placer, arrived, preferred_element_type=jnp.float32
     ).astype(jnp.bfloat16)
-    incoming = lax.all_gather(own_block, "blk", axis=2, tiled=True)
+    incoming = collect(own_block, "blk", 2)
     cross_re = jnp.einsum("xnif,xnjf->fij", own_block, incoming, preferred_element_type=jnp.float32)
     cross_im = jnp.einsum(
         "nif,njf->fij", own_block[1], incoming[0], preferred_element_type=jnp.float32

time: 165 us -> 530 us (3.21)
  local copies, waits for them, and re-layouts: 33.8 us -> 407 us
  waiting for transfers between devices: 83.7 us -> 69.4 us
  starting transfers between devices: 8.39 us -> 22.2 us
  matrix products: 16.9 us -> 8.77 us
    dynamic_update_slice x0 -> x8, local copies, waits for them, and re-layouts: none -> 362 us  [the longest x4 195 us: collect(): lax.dynamic_update_slice_in_dim(result, from_left, (here - step) % size *...]
    all_gather x1 -> x0, waiting for transfers between devices: 43.8 us -> none  [per_device(): incoming = lax.all_gather(own_block, 'blk', axis=2, tiled=True)]
    ppermute x0 -> x7, local copies, waits for them, and re-layouts: none -> 30.9 us  [the longest x4 17.3 us: collect(): from_left = lax.ppermute(from_left, axis, forward)]
    ppermute x0 -> x7, waiting for transfers between devices: none -> 20.2 us  [the longest x4 13.7 us: collect(): from_left = lax.ppermute(from_left, axis, forward)]
    ppermute x0 -> x7, starting transfers between devices: none -> 14 us  [the longest x3 10.1 us: collect(): from_right = lax.ppermute(from_right, axis, left)]
    all_gather x1 -> x0, local copies, waits for them, and re-layouts: 12.6 us -> none  [per_device(): incoming = lax.all_gather(own_block, 'blk', axis=2, tiled=True)]
    unnamed x3 -> x2, waiting for transfers between devices: 30.2 us -> 39.5 us
    squeeze x3 -> x0, local copies, waits for them, and re-layouts: 8.58 us -> none  [the longest x2 5.95 us: per_device(): incoming[1]]
  transfers between devices with their start and end apart: 5 -> 11, of which waited for: 5 -> 8; matrix products, arithmetic and copies ran while one was open for 5% -> 66% of each run, Pallas kernels for 0% -> 0%
where the time goes in v1:
time: 530 us; the launch traced here: 529 us
  local copies, waits for them, and re-layouts  407 us (77%)
  waiting for transfers between devices  69.4 us (13%)
  starting transfers between devices  22.2 us (4%)
  between operations  13.8 us (3%)
  matrix products  8.77 us (2%)
  other arithmetic  7.81 us (1%)
    dynamic_update_slice x4, local copies, waits for them, and re-layouts, collect(): lax.dynamic_update_slice_in_dim(result, from_left, (here - step) % size *...  195 us
    dynamic_update_slice x3, local copies, waits for them, and re-layouts, collect(): lax.dynamic_update_slice_in_dim(result, from_right, (here + step) % size...  146 us
    unnamed x2, waiting for transfers between devices  39.5 us
    dynamic_update_slice x1, local copies, waits for them, and re-layouts, collect(): lax.dynamic_update_slice_in_dim(result, shard, here * rows, axis=dim)  20.9 us
    ppermute x4, local copies, waits for them, and re-layouts, collect(): from_left = lax.ppermute(from_left, axis, forward)  17.3 us
    ppermute x4, waiting for transfers between devices, collect(): from_left = lax.ppermute(from_left, axis, forward)  13.7 us
    ppermute x3, local copies, waits for them, and re-layouts, collect(): from_right = lax.ppermute(from_right, axis, left)  13.6 us
  transfers between devices with their start and end apart: 11, of which 8 were waited for; matrix products, arithmetic and copies ran while one was open for 66% of the time, Pallas kernels for 0%

profile of v1, /device:TPU:0, one launch (start us, length us, event | category | flops | bytes accessed | tf_op | source)
XLA Modules:
  0.0 529.1 jit_solution(6426175619779160591)
XLA Ops:
  7.8 5.0 multiply_convert_fusion.1
  23.4 7.2 %all-to-all-start = ((bf16[8,2,2,32,128]{4,1,3,2,0:T(2,128)(2,1)}), bf16[8,2,2,32,128]{4,1,3,2,0:T(2,128)(2,1)S(1)}, u32[]{:S(2)}, u32[]{:S(2)}) async-start(bf16[8,2,2,32,128]{4,1,3,2,0:T(2,128)(2,1)} %copy.50), calls=%async_computation | async-start | bytes 524288 | tf_op jit(solution)/shard_map/all_to_all | solution.py:161
  30.8 9.0 %all-to-all-done = bf16[8,2,2,32,128]{4,1,3,2,0:T(2,128)(2,1)S(1)} async-done(((bf16[8,2,2,32,128]{4,1,3,2,0:T(2,128)(2,1)}), bf16[8,2,2,32,128]{4,1,3,2,0:T(2,128)(2,1)S(1)}, u32[]{:S(2)}, u32[]{:S(2)}) %all-to-all-start) | async-done | bytes 262176 | tf_op jit(solution)/shard_map/all_to_all | solution.py:161
  45.0 5.6 %collective-permute-done.2 = bf16[2,32,16,128]{3,2,1,0:T(8,128)(2,1)S(1)} collective-permute-done((bf16[2,32,16,128]{3,2,1,0:T(8,128)(2,1)S(1)}, bf16[2,32,16,128]{3,2,1,0:T(8,128)(2,1)S(1)}, u32[]{:S(2)}, u32[]{:S(2)}) %collective-permute-start.2) | collective-permute-done | bytes 262176 | tf_op jit(solution)/shard_map/ppermute | solution.py:25
  53.1 4.3 collective-permute-start.5
  57.3 3.7 collective-permute-done.4
  61.0 6.5 %collective-permute-done.5 = bf16[2,32,16,128]{3,2,1,0:T(8,128)(2,1)} collective-permute-done((bf16[2,32,16,128]{3,2,1,0:T(8,128)(2,1)S(1)}, bf16[2,32,16,128]{3,2,1,0:T(8,128)(2,1)}, u32[]{:S(2)}, u32[]{:S(2)}) %collective-permute-start.5) | collective-permute-done | bytes 262176 | tf_op jit(solution)/shard_map/ppermute | solution.py:30
  70.0 4.4 collective-permute-done.6
  82.4 20.9 %dynamic_update_slice.24 = bf16[2,32,128,128]{2,1,3,0:T(8,128)(2,1)S(1)} dynamic-update-slice(bf16[2,32,128,128]{2,1,3,0:T(8,128)(2,1)S(1)} %broadcast_in_dim.2, bf16[2,32,16,128]{2,1,3,0:T(8,128)(2,1)} %copy.53, s32[]{:T(128)} %constant.176.clone.1, s32[]{:T(128)} %constant.176.clone.1, s32[]{:T(128)S(6)} %select_n.234, s32[]{:T(128)} %constant.176.clone.1) | dynamic-update-slice | bytes 524292 | tf_op jit(solution)/shard_map/dynamic_update_slice | solution.py:21
  103.3 4.5 copy.54
  107.9 48.7 %dynamic_update_slice.25 = bf16[2,32,128,128]{2,1,3,0:T(8,128)(2,1)S(1)} dynamic-update-slice(bf16[2,32,128,128]{2,1,3,0:T(8,128)(2,1)S(1)} %dynamic_update_slice.24, bf16[2,32,16,128]{2,1,3,0:T(8,128)(2,1)} %copy.54, s32[]{:T(128)} %constant.176.clone.1, s32[]{:T(128)} %constant.176.clone.1, s32[]{:T(128)S(6)} %select_n.236, s32[]{:T(128)} %constant.176.clone.1) | dynamic-update-slice | bytes 524292 | tf_op jit(solution)/shard_map/dynamic_update_slice | solution.py:26
  156.5 4.5 copy.55
  161.1 48.7 %dynamic_update_slice.26 = bf16[2,32,128,128]{2,1,3,0:T(8,128)(2,1)S(1)} dynamic-update-slice(bf16[2,32,128,128]{2,1,3,0:T(8,128)(2,1)S(1)} %dynamic_update_slice.25, bf16[2,32,16,128]{2,1,3,0:T(8,128)(2,1)} %copy.55, s32[]{:T(128)} %constant.176.clone.1, s32[]{:T(128)} %constant.176.clone.1, s32[]{:T(128)S(6)} %select_n.238, s32[]{:T(128)} %constant.176.clone.1) | dynamic-update-slice | bytes 524292 | tf_op jit(solution)/shard_map/dynamic_update_slice | solution.py:31
  209.7 4.5 copy.56
  214.3 48.7 %dynamic_update_slice.27 = bf16[2,32,128,128]{2,1,3,0:T(8,128)(2,1)S(1)} dynamic-update-slice(bf16[2,32,128,128]{2,1,3,0:T(8,128)(2,1)S(1)} %dynamic_update_slice.26, bf16[2,32,16,128]{2,1,3,0:T(8,128)(2,1)} %copy.56, s32[]{:T(128)} %constant.176.clone.1, s32[]{:T(128)} %constant.176.clone.1, s32[]{:T(128)S(6)} %select_n.240, s32[]{:T(128)} %constant.176.clone.1) | dynamic-update-slice | bytes 524292 | tf_op jit(solution)/shard_map/dynamic_update_slice | solution.py:26
  262.9 4.5 copy.57
  267.5 48.7 %dynamic_update_slice.28 = bf16[2,32,128,128]{2,1,3,0:T(8,128)(2,1)S(1)} dynamic-update-slice(bf16[2,32,128,128]{2,1,3,0:T(8,128)(2,1)S(1)} %dynamic_update_slice.27, bf16[2,32,16,128]{2,1,3,0:T(8,128)(2,1)} %copy.57, s32[]{:T(128)} %constant.176.clone.1, s32[]{:T(128)} %constant.176.clone.1, s32[]{:T(128)S(6)} %select_n.242, s32[]{:T(128)} %constant.176.clone.1) | dynamic-update-slice | bytes 524292 | tf_op jit(solution)/shard_map/dynamic_update_slice | solution.py:31
  316.1 3.7 copy.58
  319.8 48.7 %dynamic_update_slice.29 = bf16[2,32,128,128]{2,1,3,0:T(8,128)(2,1)S(1)} dynamic-update-slice(bf16[2,32,128,128]{2,1,3,0:T(8,128)(2,1)S(1)} %dynamic_update_slice.28, bf16[2,32,16,128]{2,1,3,0:T(8,128)(2,1)} %copy.58, s32[]{:T(128)} %constant.176.clone.1, s32[]{:T(128)} %constant.176.clone.1, s32[]{:T(128)S(6)} %select_n.244, s32[]{:T(128)} %constant.176.clone.1) | dynamic-update-slice | bytes 524292 | tf_op jit(solution)/shard_map/dynamic_update_slice | solution.py:26
  368.5 4.5 copy.59
  373.0 48.7 %dynamic_update_slice.30 = bf16[2,32,128,128]{2,1,3,0:T(8,128)(2,1)S(1)} dynamic-update-slice(bf16[2,32,128,128]{2,1,3,0:T(8,128)(2,1)S(1)} %dynamic_update_slice.29, bf16[2,32,16,128]{2,1,3,0:T(8,128)(2,1)} %copy.59, s32[]{:T(128)} %constant.176.clone.1, s32[]{:T(128)} %constant.176.clone.1, s32[]{:T(128)S(6)} %select_n.246, s32[]{:T(128)} %constant.176.clone.1) | dynamic-update-slice | bytes 524292 | tf_op jit(solution)/shard_map/dynamic_update_slice | solution.py:31
  421.7 4.5 copy.60
  426.2 48.7 %dynamic_update_slice.31 = bf16[2,32,128,128]{2,1,3,0:T(8,128)(2,1)S(1)} dynamic-update-slice(bf16[2,32,128,128]{2,1,3,0:T(8,128)(2,1)S(1)} %dynamic_update_slice.30, bf16[2,32,16,128]{2,1,3,0:T(8,128)(2,1)} %copy.60, s32[]{:T(128)} %constant.176.clone.1, s32[]{:T(128)} %constant.176.clone.1, s32[]{:T(128)S(6)} %select_n.248, s32[]{:T(128)} %constant.176.clone.1) | dynamic-update-slice | bytes 524292 | tf_op jit(solution)/shard_map/dynamic_update_slice | solution.py:26
  480.3 39.5 %reduce-scatter.5.cloned.1.call-done = f32[64,4096]{1,0:T(8,128)} async-done(((f32[128,4096]{1,0:T(8,128)}), f32[64,4096]{1,0:T(8,128)}) %reduce-scatter.5.cloned.1.call-update) | async-done | bytes 1048592
  (79 shorter events, 37.8 us)
Async XLA Ops:
  6.5 12.6 %copy-start = (f32[128]{0:T(128)S(1)}, f32[128]{0:T(128)}, u32[]{:S(2)}) copy-start(f32[128]{0:T(128)} %param.5) | copy-start | bytes 1540
  7.8 5.0 copy-start.8
  15.6 5.8 %copy-start.6 = (s32[1,8,2]{1,2,0:T(2,128)S(1)}, s32[1,8,2]{1,2,0:T(2,128)}, u32[]{:S(2)}) copy-start(s32[1,8,2]{1,2,0:T(2,128)} %param.6) | copy-start | bytes 196
  18.5 12.1 %copy-start.7 = (s32[1,8,2]{1,2,0:T(2,128)S(1)}, s32[1,8,2]{1,2,0:T(2,128)}, u32[]{:S(2)}) copy-start(s32[1,8,2]{1,2,0:T(2,128)} %param.7) | copy-start | bytes 196
  18.6 1.7 collective-permute-start
  20.5 1.3 collective-permute-start.1
  23.4 16.4 %all-to-all-start = ((bf16[8,2,2,32,128]{4,1,3,2,0:T(2,128)(2,1)}), bf16[8,2,2,32,128]{4,1,3,2,0:T(2,128)(2,1)S(1)}, u32[]{:S(2)}, u32[]{:S(2)}) async-start(bf16[8,2,2,32,128]{4,1,3,2,0:T(2,128)(2,1)} %copy.50), calls=%async_computation | async-start | bytes 524288 | tf_op jit(solution)/shard_map/all_to_all | solution.py:161
  30.6 489.2 %reduce-scatter.5.cloned.1.call-start = ((), (), s32[]{:S(2)}) async-start(), calls=%async_computation.2 | async-start | bytes 3145728
  40.2 10.4 %collective-permute-start.2 = (bf16[2,32,16,128]{3,2,1,0:T(8,128)(2,1)S(1)}, bf16[2,32,16,128]{3,2,1,0:T(8,128)(2,1)S(1)}, u32[]{:S(2)}, u32[]{:S(2)}) collective-permute-start(bf16[2,32,16,128]{3,2,1,0:T(8,128)(2,1)S(1)} %fusion.12), channel_id=1, source_target_pairs={{0,4},{4,8},{8,12},{12,16},{16,20},{20,24},{24,28},{28,0},{1,5},{5... | collective-permute-start | bytes 786440 | tf_op jit(solution)/shard_map/ppermute | solution.py:25
  41.7 11.4 %collective-permute-start.3 = (bf16[2,32,16,128]{3,2,1,0:T(8,128)(2,1)S(1)}, bf16[2,32,16,128]{3,2,1,0:T(8,128)(2,1)S(1)}, u32[]{:S(2)}, u32[]{:S(2)}) collective-permute-start(bf16[2,32,16,128]{3,2,1,0:T(8,128)(2,1)S(1)} %fusion.12), channel_id=1, source_target_pairs={{0,28},{4,0},{8,4},{12,8},{16,12},{20,16},{24,20},{28,24},{1,29},{... | collective-permute-start | bytes 786440 | tf_op jit(solution)/shard_map/ppermute | solution.py:30
  50.6 23.8 %copy-start.5 = (bf16[2,32,16,128]{3,2,1,0:T(8,128)(2,1)}, bf16[2,32,16,128]{3,2,1,0:T(8,128)(2,1)S(1)}, u32[]{:S(2)}) copy-start(bf16[2,32,16,128]{3,2,1,0:T(8,128)(2,1)S(1)} %collective-permute-done.2) | copy-start | bytes 786436
  50.6 10.4 %collective-permute-start.4 = (bf16[2,32,16,128]{3,2,1,0:T(8,128)(2,1)S(1)}, bf16[2,32,16,128]{3,2,1,0:T(8,128)(2,1)S(1)}, u32[]{:S(2)}, u32[]{:S(2)}) collective-permute-start(bf16[2,32,16,128]{3,2,1,0:T(8,128)(2,1)S(1)} %collective-permute-done.2), channel_id=1, source_target_pairs={{0,4},{4,8},{8,12},{12,16},{16,20},{20,24},{24,28},{28,0},{1,5},{5... | collective-permute-start | bytes 786440 | tf_op jit(solution)/shard_map/ppermute | solution.py:25
  53.1 25.0 %copy-start.3 = (bf16[2,32,16,128]{3,2,1,0:T(8,128)(2,1)}, bf16[2,32,16,128]{3,2,1,0:T(8,128)(2,1)S(1)}, u32[]{:S(2)}) copy-start(bf16[2,32,16,128]{3,2,1,0:T(8,128)(2,1)S(1)} %collective-permute-done.3) | copy-start | bytes 786436
  53.1 14.4 %collective-permute-start.5 = (bf16[2,32,16,128]{3,2,1,0:T(8,128)(2,1)S(1)}, bf16[2,32,16,128]{3,2,1,0:T(8,128)(2,1)}, u32[]{:S(2)}, u32[]{:S(2)}) collective-permute-start(bf16[2,32,16,128]{3,2,1,0:T(8,128)(2,1)S(1)} %collective-permute-done.3), channel_id=1, source_target_pairs={{0,28},{4,0},{8,4},{12,8},{16,12},{20,16},{24,20},{28,24},{1,29},{... | collective-permute-start | bytes 786440 | tf_op jit(solution)/shard_map/ppermute | solution.py:30
  61.0 19.8 %copy-start.4 = (bf16[2,32,16,128]{3,2,1,0:T(8,128)(2,1)}, bf16[2,32,16,128]{3,2,1,0:T(8,128)(2,1)S(1)}, u32[]{:S(2)}) copy-start(bf16[2,32,16,128]{3,2,1,0:T(8,128)(2,1)S(1)} %collective-permute-done.4) | copy-start | bytes 786436
  61.0 13.4 %collective-permute-start.6 = (bf16[2,32,16,128]{3,2,1,0:T(8,128)(2,1)S(1)}, bf16[2,32,16,128]{3,2,1,0:T(8,128)(2,1)S(1)}, u32[]{:S(2)}, u32[]{:S(2)}) collective-permute-start(bf16[2,32,16,128]{3,2,1,0:T(8,128)(2,1)S(1)} %collective-permute-done.4), channel_id=1, source_target_pairs={{0,4},{4,8},{8,12},{12,16},{16,20},{20,24},{24,28},{28,0},{1,5},{5... | collective-permute-start | bytes 786440 | tf_op jit(solution)/shard_map/ppermute | solution.py:25
  67.5 300.9 %collective-permute-start.7 = (bf16[2,32,16,128]{3,2,1,0:T(8,128)(2,1)}, bf16[2,32,16,128]{3,2,1,0:T(8,128)(2,1)}, u32[]{:S(2)}, u32[]{:S(2)}) collective-permute-start(bf16[2,32,16,128]{3,2,1,0:T(8,128)(2,1)} %collective-permute-done.5), channel_id=1, source_target_pairs={{0,28},{4,0},{8,4},{12,8},{16,12},{20,16},{24,20},{28,24},{1,29},{... | collective-permute-start | bytes 786440 | tf_op jit(solution)/shard_map/ppermute | solution.py:30
  74.4 347.3 %collective-permute-start.8 = (bf16[2,32,16,128]{3,2,1,0:T(8,128)(2,1)S(1)}, bf16[2,32,16,128]{3,2,1,0:T(8,128)(2,1)}, u32[]{:S(2)}, u32[]{:S(2)}) collective-permute-start(bf16[2,32,16,128]{3,2,1,0:T(8,128)(2,1)S(1)} %collective-permute-done.6), channel_id=1, source_target_pairs={{0,4},{4,8},{8,12},{12,16},{16,20},{20,24},{24,28},{28,0},{1,5},{5... | collective-permute-start | bytes 786440 | tf_op jit(solution)/shard_map/ppermute | solution.py:25
  474.9 1.0 copy-start.1
  474.9 1.5 copy-start.2
Sparse Core Ops, SparseCore 0:
  480.4 39.3 reduce-scatter.4
